TPU v7x, 128 devices: a whole 4x4x4 slice. The times are simulated.
128 devices in a mesh: row: 8 (over z, core), col: 16 (over x, y).
Axes of the slice: x: 4, y: 4, z: 4, core: 2. Of those that a mesh axis runs over, the one named last changes fastest.
Arguments:
- tokens: bfloat16 [4096, 2048], P('col', 'row'), may hold values from -6 to 6
- router: bfloat16 [2048, 32], replicated, may hold values from -0.125 to 0.125
- shared_gate_vector: bfloat16 [2048], replicated, may hold values from -0.125 to 0.125
- shared_gate_weight: bfloat16 [2048, 5632], P('col', 'row'), may hold values from -0.125 to 0.125
- shared_up_weight: bfloat16 [2048, 5632], P('col', 'row'), may hold values from -0.125 to 0.125
- shared_down_weight: bfloat16 [5632, 2048], P('row', 'col'), may hold values from -0.078125 to 0.078125
- routed_gate_weight: bfloat16 [32, 2048, 1408], P('col', None, 'row'), may hold values from -0.125 to 0.125
- routed_up_weight: bfloat16 [32, 2048, 1408], P('col', None, 'row'), may hold values from -0.125 to 0.125
- routed_down_weight: bfloat16 [32, 1408, 2048], P('col', 'row'), may hold values from -0.15625 to 0.15625
- adapter_input_factor: bfloat16 [64, 16, 2048], P(None, None, 'row'), may hold values from -0.125 to 0.125
- adapter_output_factor: bfloat16 [64, 16, 5632], P(None, None, 'row'), may hold values from -0.29882812 to 0.29882812
- routes: int32 [4096, 4], P('col'), may hold values from 0 to 31, all different within a row; in each aligned block of 256 rows (0 to 255, 256 to 511, ...) at most 64 rows name the same one
- lengths: int32 [16, 16], P('col'), may hold values from 1 to 128, 256 in all within a row
- prompt_adapter_index: int32 [16, 16], P('col'), may hold values from 0 to 15
- active_adapter_index: int32 [16], replicated, may hold values from 0 to 63, as said below
Outputs:
- moe_out: float32 [4096, 2048], P('col', 'row')
Inputs may be any that keep to these rules, and one draw needn't show every extreme that they name: `routes`: in each group of 256 consecutive tokens no expert is named by more than 64 tokens, a bound that some block reaches. Each group's 16 lengths sum to 256; the longest is exactly 128. `active_adapter_index`: the 16 entries are distinct.
All inputs are finite; a program needn't handle non-finite values.
Results may differ from a plain program's by a relative error of at most 0.003.
Values may be sent and summed in bfloat16 or wider, within the bound.
No kernel may reach another device: no remote copies, remote signals or barrier semaphores. Data moves between devices by JAX's collectives and lax.ppermute only.
A program may use at most 128 MiB of HBM per device.

v0:
```python
import jax
import jax.numpy as jnp
from jax import lax
from jax.sharding import PartitionSpec as P

ADAPTER_SCALE = 2.0


def on_device(
    tokens,
    router,
    shared_gate_vector,
    shared_gate_weight,
    shared_up_weight,
    shared_down_weight,
    routed_gate_weight,
    routed_up_weight,
    routed_down_weight,
    adapter_input_factor,
    adapter_output_factor,
    routes,
    lengths,
    prompt_adapter_index,
    active_adapter_index,
):
    all_features = lax.all_gather(tokens, "row", axis=1, tiled=True)
    token_count = all_features.shape[0]
    full_width = all_features.shape[1]
    local_width = tokens.shape[1]
    col_count = lax.axis_size("col")
    local_experts = routed_gate_weight.shape[0]
    expert_count = local_experts * col_count
    route_count = routes.shape[1]
    capacity = 2 * token_count * route_count // expert_count
    logits = jnp.dot(all_features, router, preferred_element_type=jnp.float32)
    onehot = routes[:, :, None] == jnp.arange(expert_count, dtype=jnp.int32)[None, None, :]
    picked = jnp.sum(jnp.where(onehot, logits[:, None, :], 0.0), axis=2)
    raw_exp = jnp.exp(picked)
    gate_weights = raw_exp / jnp.sum(raw_exp, axis=1, keepdims=True)
    share = jax.nn.sigmoid(
        jnp.dot(all_features, shared_gate_vector, preferred_element_type=jnp.float32)
    )
    hit_table = jnp.any(onehot, axis=1).astype(jnp.int32)
    running_count = jnp.cumsum(hit_table, axis=0)
    slot_rank = running_count - hit_table
    route_rank = jnp.sum(jnp.where(onehot, slot_rank[:, None, :], 0), axis=2)
    row_index = routes * capacity + route_rank
    request_ends = jnp.cumsum(lengths[0])
    request_count = lengths.shape[1]
    token_position = jnp.arange(token_count, dtype=jnp.int32)
    request_of = jnp.sum(
        (token_position[:, None] >= request_ends[None, :]).astype(jnp.int32), axis=1
    )
    request_match = request_of[:, None] == jnp.arange(request_count, dtype=jnp.int32)[None, :]
    adapter_of = jnp.sum(jnp.where(request_match, prompt_adapter_index[0][None, :], 0), axis=1)
    picked_input_factor = jnp.take(adapter_input_factor, active_adapter_index, axis=0)
    rank_width = picked_input_factor.shape[1]
    reduced_rank_value = picked_input_factor.shape[0] * rank_width
    full_in = lax.all_gather(picked_input_factor, "row", axis=2, tiled=True).reshape(
        reduced_rank_value, full_width
    )
    low_rank = lax.dot_general(
        all_features, full_in, (((1,), (1,)), ((), ())), preferred_element_type=jnp.float32
    )
    owner = jnp.arange(reduced_rank_value, dtype=jnp.int32) // rank_width
    adapter_mask = adapter_of[:, None] == owner[None, :]
    low_masked = jnp.where(adapter_mask, low_rank.astype(jnp.bfloat16), jnp.zeros((), jnp.bfloat16))
    picked_output_factor = jnp.take(adapter_output_factor, active_adapter_index, axis=0).reshape(
        reduced_rank_value, adapter_output_factor.shape[2]
    )
    adapter_update = jnp.dot(low_masked, picked_output_factor, preferred_element_type=jnp.float32)
    shared_gate_value = jnp.dot(
        all_features,
        lax.all_gather(shared_gate_weight, "col", axis=0, tiled=True),
        preferred_element_type=jnp.float32,
    )
    shared_up_value = jnp.dot(
        all_features,
        lax.all_gather(shared_up_weight, "col", axis=0, tiled=True),
        preferred_element_type=jnp.float32,
    )
    shared_hidden_units = (
        jax.nn.silu(shared_gate_value) * (shared_up_value + ADAPTER_SCALE * adapter_update)
    ).astype(jnp.bfloat16)
    shared_part = jnp.dot(
        shared_hidden_units,
        lax.all_gather(shared_down_weight, "col", axis=1, tiled=True),
        preferred_element_type=jnp.float32,
    )
    shared_part = shared_part * share[:, None]
    positions = jnp.arange(capacity, dtype=jnp.int32)
    slot_token = jnp.sum(
        (running_count.T[:, None, :] <= positions[None, :, None]).astype(jnp.int32), axis=2
    )
    slot_valid = positions[None, :] < running_count[-1][:, None]
    picked_rows = jnp.take(all_features, jnp.minimum(slot_token, token_count - 1), axis=0)
    chosen = jnp.where(slot_valid[:, :, None], picked_rows, jnp.zeros((), jnp.bfloat16))
    outgoing = chosen.reshape(col_count, local_experts, capacity, full_width)
    slot_block = lax.all_to_all(outgoing, "col", split_axis=0, concat_axis=0, tiled=True)
    gate_part = jnp.einsum(
        "sexd,edf->sexf", slot_block, routed_gate_weight, preferred_element_type=jnp.float32
    )
    up_part = jnp.einsum(
        "sexd,edf->sexf", slot_block, routed_up_weight, preferred_element_type=jnp.float32
    )
    hidden = (jax.nn.silu(gate_part) * up_part).astype(jnp.bfloat16)
    partial_value = jnp.einsum(
        "sexf,efd->sexd", hidden, routed_down_weight, preferred_element_type=jnp.float32
    )
    summed, shared_sum = (
        lax.psum_scatter(partial_value, "row", scatter_dimension=3, tiled=True),
        lax.psum_scatter(shared_part, "row", scatter_dimension=1, tiled=True),
    )
    returned = lax.all_to_all(summed, "col", split_axis=0, concat_axis=0, tiled=True)
    flat_rows = returned.reshape(expert_count * capacity, local_width)
    routed_rows = jnp.take(flat_rows, row_index, axis=0)
    routed = jnp.sum(gate_weights[:, :, None] * routed_rows, axis=1)
    return routed + shared_sum


def solution(mesh):
    return jax.shard_map(
        on_device,
        mesh=mesh,
        in_specs=(
            P("col", "row"),
            P(),
            P(),
            P("col", "row"),
            P("col", "row"),
            P("row", "col"),
            P("col", None, "row"),
            P("col", None, "row"),
            P("col", "row", None),
            P(None, None, "row"),
            P(None, None, "row"),
            P("col", None),
            P("col", None),
            P("col", None),
            P(),
        ),
        out_specs=P("col", "row"),
        check_vma=False,
    )
```

profile of v0, /device:TPU:0, one launch (start us, length us, event | category | flops | bytes accessed | tf_op | source)
XLA Modules:
  0.0 487.8 jit_solution(12929686134690936716)
XLA Ops:
  6.5 0.7 all-gather.6.cloned.1.call-update
  7.3 0.0 all-gather.12.cloned.1.call-start
  7.3 0.7 compare_select_fusion.3
  8.0 1.6 gather_fusion.2
  9.6 0.7 compare_and_fusion.2
  10.2 0.7 broadcast_select_fusion
  11.0 0.0 all-gather.8.cloned.1.call-start
  11.1 0.7 all-gather.8.cloned.1.call-update
  11.8 0.0 all-gather.10.cloned.1.call-start
  11.8 0.5 all-gather.10.cloned.1.call-update
  12.3 0.7 fusion.29
  13.1 0.6 reduce-window.18
  13.7 0.2 slice_reduce_fusion
  13.9 0.1 fusion.33
  14.0 0.6 convert_reduce_fusion
  14.6 0.2 slice_reduce_fusion.1
  14.8 0.1 lt.58
  14.9 0.1 reshape.157
  15.0 0.1 compare_and_fusion
  15.1 20.0 %all-gather.6.cloned.1.call-done = bf16[256,2048]{1,0:T(8,128)(2,1)} async-done(((bf16[256,256]{1,0:T(8,128)(2,1)}), bf16[256,2048]{1,0:T(8,128)(2,1)}) %all-gather.6.cloned.1.call-update) | async-done | bytes 1048592 | tf_op jit(solution)/shard_map/all_gather | solution.py:26
  35.0 17.7 %gather_fusion = bf16[2048,2048]{1,0:T(8,128)(2,1)} fusion(bf16[256,2048]{1,0:T(8,128)(2,1)} %all-gather.6.cloned.1.call-done, s32[2048]{0:T(1024)S(1)} %broadcast_clamp_fusion), kind=kCustom, calls=%fused_computation | custom fusion | bytes 16785408 | tf_op jit(solution)/shard_map/jit(_take)/gather | solution.py:96
  52.7 7.5 %select_select_fusion = bf16[16,2,64,2048]{3,2,1,0:T(8,128)(2,1)} fusion(bf16[16,2,64,2048]{3,2,1,0:T(8,128)(2,1)} %bitcast.88, pred[16,2,64]{2,1,0:T(4,128)(4,1)S(1)} %get-tuple-element.9, pred[16,2,64]{2,1,0:T(4,128)(4,1)S(1)} %get-tuple-element.10), kind=kLoop, calls=%fused_computation.4 | loop fusion | flops 8388608 | bytes 16781312 | tf_op jit(solution)/shard_map/jit(_where)/select_n | solution.py:97
  60.2 7.0 %all-to-all-start = ((bf16[16,2,64,2048]{3,2,1,0:T(8,128)(2,1)}), bf16[16,2,64,2048]{3,2,1,0:T(8,128)(2,1)}, u32[]{:S(2)}, u32[]{:S(2)}) async-start(bf16[16,2,64,2048]{3,2,1,0:T(8,128)(2,1)} %select_select_fusion), calls=%async_computation | async-start | bytes 16777216 | tf_op jit(solution)/shard_map/all_to_all | solution.py:99
  67.2 0.0 all-gather.14.cloned.1.call-start
  67.3 0.5 all-gather.14.cloned.1.call-update
  67.8 0.0 reduce-scatter.3.cloned.1.call-start
  67.9 152.1 %all-to-all-done = bf16[16,2,64,2048]{3,2,1,0:T(8,128)(2,1)} async-done(((bf16[16,2,64,2048]{3,2,1,0:T(8,128)(2,1)}), bf16[16,2,64,2048]{3,2,1,0:T(8,128)(2,1)}, u32[]{:S(2)}, u32[]{:S(2)}) %all-to-all-start) | async-done | bytes 8388640 | tf_op jit(solution)/shard_map/all_to_all | solution.py:99
  219.9 7.0 %fusion.2 = f32[2,16,64,176]{3,2,1,0:T(8,128)} fusion(bf16[16,2,64,2048]{3,2,1,0:T(8,128)(2,1)} %all-to-all-done, bf16[2,2048,176]{1,2,0:T(8,128)(2,1)S(1)} %copy-done.7), kind=kOutput, calls=%fused_computation.7 | convolution fusion | flops 1476395008 | bytes 11272192 | tf_op jit(solution)/shard_map/sexd,edf->sexf/dot_general | solution.py:100
  227.0 15.2 %convolution_bitcast_fusion = f32[16,2,64,2048]{3,2,0,1:T(8,128)} fusion(f32[2,16,64,176]{3,2,1,0:T(8,128)} %fusion.2, bf16[16,2,64,2048]{3,2,1,0:T(8,128)(2,1)} %all-to-all-done, bf16[2,176,2048]{2,1,0:T(8,128)(2,1)} %param.23, bf16[2,2048,176]{1,2,0:T(8,128)(2,1)} %param.22), kind=kOutput, calls=%fused_computation.9 | convolution fusion | flops 2954952704 | bytes 29491200 | tf_op jit(solution)/shard_map/sexf,efd->sexd/dot_general | solution.py:107
  242.2 0.0 reduce-scatter.3.cloned.1.call-update
  242.2 0.2 reduce-scatter.5.cloned.1.call-start
  242.4 0.1 broadcast_in_dim.137
  242.5 0.1 broadcast_in_dim.138
  242.6 0.3 copy-done.4
  242.9 0.1 copy.54
  243.0 0.1 reduce.2
  243.1 0.6 gather_fusion.3
  243.7 0.1 convert_reduce_fusion.1
  243.8 0.1 select_reduce_fusion.2
  243.9 0.1 bitcast_select_fusion
  244.0 0.4 fusion.37
  244.4 0.0 all-gather.12.cloned.1.call-done
  244.4 1.7 fusion.20
  246.2 0.0 all-gather.8.cloned.1.call-done
  246.2 3.6 fusion.35
  249.8 35.6 %all-gather.10.cloned.1.call-done = bf16[2048,704]{0,1:T(8,128)(2,1)} async-done(((bf16[128,704]{0,1:T(8,128)(2,1)}), bf16[2048,704]{0,1:T(8,128)(2,1)}) %all-gather.10.cloned.1.call-update) | async-done | bytes 2883600 | tf_op jit(solution)/shard_map/all_gather | solution.py:79
  285.5 3.6 fusion.36
  289.1 48.2 %all-gather.14.cloned.1.call-done = bf16[704,2048]{1,0:T(8,128)(2,1)} async-done(((bf16[704,128]{1,0:T(8,128)(2,1)}), bf16[704,2048]{1,0:T(8,128)(2,1)}) %all-gather.14.cloned.1.call-update) | async-done | bytes 2883600 | tf_op jit(solution)/shard_map/all_gather | solution.py:87
  337.3 4.9 %convolution_multiply_fusion = f32[256,2048]{1,0:T(8,128)} fusion(bf16[704,2048]{1,0:T(8,128)(2,1)} %all-gather.14.cloned.1.call-done, f32[256,704]{0,1:T(8,128)} %fusion.36, bf16[256,256]{0,1:T(8,128)(2,1)S(1)} %fusion.20, bf16[256,704]{1,0:T(8,128)(2,1)S(1)} %bitcast_select_fusion, f32[256]{0:T(256)S(1)} %add_divide_fusion, f32[256,704]{0,1:T(8,128)} %fusion.35), kind=kOutput, calls=%fused_computation.10 | convolution fusion | flops 832438272 | bytes 6915072 | tf_op jit(solution)/shard_map/dot_general | solution.py:85
  342.2 88.8 %reduce-scatter.3.cloned.1.call-done = f32[16,2,64,256]{3,2,0,1:T(8,128)} async-done(((f32[16,2,64,2048]{3,2,0,1:T(8,128)}), f32[16,2,64,256]{3,2,0,1:T(8,128)}) %reduce-scatter.3.cloned.1.call-update) | async-done | bytes 2097168 | tf_op jit(solution)/shard_map/reduce_scatter | solution.py:111
  431.0 3.2 copy.52
  434.2 7.0 %all-to-all-start.1 = ((f32[16,2,64,256]{3,2,1,0:T(8,128)}), f32[16,2,64,256]{3,2,1,0:T(8,128)}, u32[]{:S(2)}, u32[]{:S(2)}) async-start(f32[16,2,64,256]{3,2,1,0:T(8,128)} %copy.52), calls=%async_computation.2 | async-start | bytes 4194304 | tf_op jit(solution)/shard_map/all_to_all | solution.py:114
  441.2 0.1 convert_subtract_fusion
  441.3 0.2 copy.49
  441.5 0.1 copy.53
  441.7 0.1 reshape.165
  441.8 0.4 fusion.34
  442.3 0.1 copy.46
  442.5 27.9 %all-to-all-done.1 = f32[16,2,64,256]{3,2,1,0:T(8,128)} async-done(((f32[16,2,64,256]{3,2,1,0:T(8,128)}), f32[16,2,64,256]{3,2,1,0:T(8,128)}, u32[]{:S(2)}, u32[]{:S(2)}) %all-to-all-start.1) | async-done | bytes 2097184 | tf_op jit(solution)/shard_map/all_to_all | solution.py:114
  470.3 5.1 %gather_fusion.1 = f32[1024,256]{1,0:T(8,128)S(1)} fusion(f32[2048,256]{1,0:T(8,128)} %bitcast.14, s32[1024]{0:T(1024)S(1)} %broadcast_clamp_fusion.1), kind=kCustom, calls=%fused_computation.1 | custom fusion | bytes 2101248 | tf_op jit(solution)/shard_map/jit(_take)/gather | solution.py:116
  475.4 1.3 reshape.164
  476.7 2.5 multiply_reduce_fusion
  479.2 0.0 reduce-scatter.5.cloned.1.call-done
  479.2 1.7 add.77
  (35 shorter events, 0.3 us)
Async XLA Ops:
  6.5 236.6 %copy-start = (bf16[64,16,704]{2,1,0:T(8,128)(2,1)S(1)}, bf16[64,16,704]{2,1,0:T(8,128)(2,1)}, u32[]{:S(2)}) copy-start(bf16[64,16,704]{2,1,0:T(8,128)(2,1)} %param.25) | copy-start | bytes 4325380
  6.5 28.5 %all-gather.6.cloned.1.call-start = ((), (), s32[]{:S(2)}) async-start(), calls=%async_computation.4 | async-start | bytes 1179648 | tf_op jit(solution)/shard_map/all_gather | solution.py:26
  7.3 237.2 %all-gather.12.cloned.1.call-start = ((), (), s32[]{:S(2)}) async-start(), calls=%async_computation.8 | async-start | bytes 1179648 | tf_op jit(solution)/shard_map/all_gather | solution.py:59
  11.0 235.2 %all-gather.8.cloned.1.call-start = ((), (), s32[]{:S(2)}) async-start(), calls=%async_computation.6 | async-start | bytes 3063808 | tf_op jit(solution)/shard_map/all_gather | solution.py:74
  11.8 273.7 %all-gather.10.cloned.1.call-start = ((), (), s32[]{:S(2)}) async-start(), calls=%async_computation.7 | async-start | bytes 3063808 | tf_op jit(solution)/shard_map/all_gather | solution.py:79
  60.2 159.7 %copy-start.7 = (bf16[2,2048,176]{1,2,0:T(8,128)(2,1)S(1)}, bf16[2,2048,176]{1,2,0:T(8,128)(2,1)}, u32[]{:S(2)}) copy-start(bf16[2,2048,176]{1,2,0:T(8,128)(2,1)} %param.21) | copy-start | bytes 4325380
  60.2 159.7 %all-to-all-start = ((bf16[16,2,64,2048]{3,2,1,0:T(8,128)(2,1)}), bf16[16,2,64,2048]{3,2,1,0:T(8,128)(2,1)}, u32[]{:S(2)}, u32[]{:S(2)}) async-start(bf16[16,2,64,2048]{3,2,1,0:T(8,128)(2,1)} %select_select_fusion), calls=%async_computation | async-start | bytes 16777216 | tf_op jit(solution)/shard_map/all_to_all | solution.py:99
  67.2 270.1 %all-gather.14.cloned.1.call-start = ((), (), s32[]{:S(2)}) async-start(), calls=%async_computation.9 | async-start | bytes 3063808 | tf_op jit(solution)/shard_map/all_gather | solution.py:87
  67.8 363.2 %reduce-scatter.3.cloned.1.call-start = ((), (), s32[]{:S(2)}) async-start(), calls=%async_computation.5 | async-start | bytes 18874368 | tf_op jit(solution)/shard_map/reduce_scatter | solution.py:111
  242.2 0.7 copy-start.4
  242.2 0.7 copy-start.5
  242.2 1.6 copy-start.6
  242.2 1.8 copy-start.1
  242.2 237.0 %reduce-scatter.5.cloned.1.call-start = ((), (), s32[]{:S(2)}) async-start(), calls=%async_computation.10 | async-start | bytes 2359296 | tf_op jit(solution)/shard_map/reduce_scatter | solution.py:112
  434.2 7.1 %copy-start.3 = (s32[256,4]{0,1:T(4,128)S(1)}, s32[256,4]{0,1:T(4,128)}, u32[]{:S(2)}) copy-start(s32[256,4]{0,1:T(4,128)} %param.26) | copy-start | bytes 12292
  434.2 7.6 %copy-start.2 = (bf16[2048,32]{0,1:T(8,128)(2,1)S(1)}, bf16[2048,32]{0,1:T(8,128)(2,1)}, u32[]{:S(2)}) copy-start(bf16[2048,32]{0,1:T(8,128)(2,1)} %param.16) | copy-start | bytes 393220
  434.2 36.1 %all-to-all-start.1 = ((f32[16,2,64,256]{3,2,1,0:T(8,128)}), f32[16,2,64,256]{3,2,1,0:T(8,128)}, u32[]{:S(2)}, u32[]{:S(2)}) async-start(f32[16,2,64,256]{3,2,1,0:T(8,128)} %copy.52), calls=%async_computation.2 | async-start | bytes 4194304 | tf_op jit(solution)/shard_map/all_to_all | solution.py:114
Sparse Core Ops, SparseCore 0:
  9.0 25.9 all-gather.5
  36.7 24.2 all-gather.11
  63.1 155.2 all-gather.7
  220.5 64.9 all-gather.9
  287.4 49.8 all-gather.13
  339.6 91.3 reduce-scatter.2
  433.4 34.4 reduce-scatter.4
where the time goes:
time: 488 us
  waiting for transfers between devices  375 us (77%)
  matrix products  36.9 us (8%)
  local copies, waits for them, and re-layouts  31 us (6%)
  other arithmetic  16.6 us (3%)
  starting transfers between devices  14.4 us (3%)
  between operations  13.7 us (3%)
    all_to_all x1, waiting for transfers between devices, on_device(): lax.all_to_all(outgoing, 'col', split_axis=0, concat_axis=0, tiled=True)  152 us
    reduce_scatter x1, waiting for transfers between devices, on_device(): lax.psum_scatter(partial_value, 'row', scatter_dimension=3, tiled=True)  88.8 us
    all_gather x1, waiting for transfers between devices, on_device(): lax.all_gather(shared_down_weight, 'col', axis=1, tiled=True)  48.2 us
    all_gather x1, waiting for transfers between devices, on_device(): lax.all_gather(shared_up_weight, 'col', axis=0, tiled=True)  35.6 us
    all_to_all x1, waiting for transfers between devices, on_device(): lax.all_to_all(summed, 'col', split_axis=0, concat_axis=0, tiled=True)  27.9 us
    all_gather x1, waiting for transfers between devices, on_device(): all_features = lax.all_gather(tokens, 'row', axis=1, tiled=True)  20 us
    gather x1, local copies, waits for them, and re-layouts, on_device(): jnp.take(all_features, jnp.minimum(slot_token, token_count - 1), axis=0)  17.7 us
    dot_general x1, matrix products, on_device(): jnp.einsum('sexf,efd->sexd', hidden, routed_down_weight, preferred_elemen...  15.2 us
  transfers between devices with their start and end apart: 9, of which 6 were waited for; matrix products, arithmetic and copies ran while one was open for 17% of the time, Pallas kernels for 0%

commit v1 on v0

--- a/solution.py
+++ b/solution.py
@@ -23,7 +23,9 @@
     prompt_adapter_index,
     active_adapter_index,
 ):
-    all_features = lax.all_gather(tokens, "row", axis=1, tiled=True)
+    all_features = jnp.concatenate(
+        lax.all_to_all(jnp.stack([tokens] * lax.axis_size("row")), "row", 0, 0), axis=1
+    )
     token_count = all_features.shape[0]
     full_width = all_features.shape[1]
     local_width = tokens.shape[1]

time: 488 us -> 452 us (0.926)
  waiting for transfers between devices: 375 us -> 335 us
  starting transfers between devices: 14.4 us -> 19.9 us
    all_gather x1, waiting for transfers between devices: 35.6 us -> 0.02 us  [on_device(): lax.all_gather(shared_up_weight, 'col', axis=0, tiled=True)]
    all_gather x1 -> x0, waiting for transfers between devices: 20 us -> none  [on_device(): all_features = lax.all_gather(tokens, 'row', axis=1, tiled=True)]
    all_to_all x0 -> x1, waiting for transfers between devices: none -> 16.1 us  [on_device(): lax.all_to_all(jnp.stack([tokens] * lax.axis_size('row')), 'row', 0, 0)]
    all_gather x1, waiting for transfers between devices: 0.02 us -> 8.27 us  [on_device(): lax.all_gather(shared_gate_weight, 'col', axis=0, tiled=True)]
    all_to_all x1, waiting for transfers between devices: 152 us -> 144 us  [on_device(): lax.all_to_all(outgoing, 'col', split_axis=0, concat_axis=0, tiled=True)]
    gather x1, local copies, waits for them, and re-layouts: 17.7 us -> 11 us  [on_device(): jnp.take(all_features, jnp.minimum(slot_token, token_count - 1), axis=0)]
    all_to_all x0 -> x1, starting transfers between devices: none -> 5.43 us  [on_device(): lax.all_to_all(jnp.stack([tokens] * lax.axis_size('row')), 'row', 0, 0)]
where the time goes in v1:
time: 452 us; the launch traced here: 451 us
  waiting for transfers between devices  335 us (74%)
  matrix products  37.5 us (8%)
  local copies, waits for them, and re-layouts  28.6 us (6%)
  starting transfers between devices  19.9 us (4%)
  other arithmetic  16 us (4%)
  between operations  13.7 us (3%)
    all_to_all x1, waiting for transfers between devices, on_device(): lax.all_to_all(outgoing, 'col', split_axis=0, concat_axis=0, tiled=True)  144 us
    reduce_scatter x1, waiting for transfers between devices, on_device(): lax.psum_scatter(partial_value, 'row', scatter_dimension=3, tiled=True)  88.8 us
    all_gather x1, waiting for transfers between devices, on_device(): lax.all_gather(shared_down_weight, 'col', axis=1, tiled=True)  48.2 us
    all_to_all x1, waiting for transfers between devices, on_device(): lax.all_to_all(summed, 'col', split_axis=0, concat_axis=0, tiled=True)  27.9 us
    all_to_all x1, waiting for transfers between devices, on_device(): lax.all_to_all(jnp.stack([tokens] * lax.axis_size('row')), 'row', 0, 0)  16.1 us
    dot_general x1, matrix products, on_device(): jnp.einsum('sexf,efd->sexd', hidden, routed_down_weight, preferred_elemen...  15.3 us
    gather x1, local copies, waits for them, and re-layouts, on_device(): jnp.take(all_features, jnp.minimum(slot_token, token_count - 1), axis=0)  11 us
  transfers between devices with their start and end apart: 9, of which 6 were waited for; matrix products, arithmetic and copies ran while one was open for 17% of the time, Pallas kernels for 0%

profile of v1, /device:TPU:0, one launch (start us, length us, event | category | flops | bytes accessed | tf_op | source)
XLA Modules:
  0.0 451.1 jit_solution(3308045273963713759)
XLA Ops:
  6.5 0.8 compare_and_fusion.2
  7.3 0.7 compare_select_fusion.3
  8.0 1.6 gather_fusion.2
  9.6 0.7 broadcast_select_fusion
  10.4 0.0 all-gather.7.cloned.1.call-start
  10.4 0.7 all-gather.7.cloned.1.call-update
  11.1 1.9 stack.2
  13.1 5.4 %all-to-all-start = ((bf16[8,256,256]{2,1,0:T(8,128)(2,1)}), bf16[8,256,256]{2,1,0:T(8,128)(2,1)S(1)}, u32[]{:S(2)}, u32[]{:S(2)}) async-start(bf16[8,256,256]{2,1,0:T(8,128)(2,1)} %stack.2), calls=%async_computation | async-start | bytes 2097152 | tf_op jit(solution)/shard_map/all_to_all | solution.py:27
  18.5 0.0 all-gather.5.cloned.1.call-start
  18.5 0.7 all-gather.5.cloned.1.call-update
  19.3 0.6 reduce-window.18
  19.9 0.2 slice_reduce_fusion
  20.1 0.1 fusion.33
  20.2 0.6 convert_reduce_fusion
  20.8 0.2 slice_reduce_fusion.1
  21.0 0.1 lt.58
  21.1 0.1 reshape.167
  21.2 0.1 compare_and_fusion
  21.3 16.1 %all-to-all-done = bf16[8,256,256]{2,1,0:T(8,128)(2,1)S(1)} async-done(((bf16[8,256,256]{2,1,0:T(8,128)(2,1)}), bf16[8,256,256]{2,1,0:T(8,128)(2,1)S(1)}, u32[]{:S(2)}, u32[]{:S(2)}) %all-to-all-start) | async-done | bytes 1048608 | tf_op jit(solution)/shard_map/all_to_all | solution.py:27
  37.3 1.0 copy-done.1
  38.3 1.3 copy.61
  39.7 11.0 %gather_fusion = bf16[2048,2048]{1,0:T(8,128)(2,1)} fusion(bf16[256,2048]{1,0:T(8,128)(2,1)S(1)} %bitcast.91, s32[2048]{0:T(1024)S(1)} %broadcast_clamp_fusion), kind=kCustom, calls=%fused_computation | custom fusion | bytes 16785408 | tf_op jit(solution)/shard_map/jit(_take)/gather | solution.py:98
  50.7 7.4 %select_select_fusion = bf16[16,2,64,2048]{3,2,1,0:T(8,128)(2,1)} fusion(bf16[16,2,64,2048]{3,2,1,0:T(8,128)(2,1)} %bitcast.97, pred[16,2,64]{2,1,0:T(4,128)(4,1)S(1)} %get-tuple-element.9, pred[16,2,64]{2,1,0:T(4,128)(4,1)S(1)} %get-tuple-element.10), kind=kLoop, calls=%fused_computation.4 | loop fusion | flops 8388608 | bytes 16781312 | tf_op jit(solution)/shard_map/jit(_where)/select_n | solution.py:99
  58.2 7.1 %all-to-all-start.1 = ((bf16[16,2,64,2048]{3,2,1,0:T(8,128)(2,1)}), bf16[16,2,64,2048]{3,2,1,0:T(8,128)(2,1)}, u32[]{:S(2)}, u32[]{:S(2)}) async-start(bf16[16,2,64,2048]{3,2,1,0:T(8,128)(2,1)} %select_select_fusion), calls=%async_computation.1 | async-start | bytes 16777216 | tf_op jit(solution)/shard_map/all_to_all | solution.py:101
  65.3 0.0 all-gather.11.cloned.1.call-start
  65.3 0.5 all-gather.11.cloned.1.call-update
  65.8 0.0 reduce-scatter.3.cloned.1.call-start
  65.9 144.2 %all-to-all-done.1 = bf16[16,2,64,2048]{3,2,1,0:T(8,128)(2,1)} async-done(((bf16[16,2,64,2048]{3,2,1,0:T(8,128)(2,1)}), bf16[16,2,64,2048]{3,2,1,0:T(8,128)(2,1)}, u32[]{:S(2)}, u32[]{:S(2)}) %all-to-all-start.1) | async-done | bytes 8388640 | tf_op jit(solution)/shard_map/all_to_all | solution.py:101
  210.1 7.4 %fusion.2 = f32[2,16,64,176]{3,2,1,0:T(8,128)} fusion(bf16[16,2,64,2048]{3,2,1,0:T(8,128)(2,1)} %all-to-all-done.1, bf16[2,2048,176]{1,2,0:T(8,128)(2,1)} %param.21), kind=kOutput, calls=%fused_computation.7 | convolution fusion | flops 1476395008 | bytes 11272192 | tf_op jit(solution)/shard_map/sexd,edf->sexf/dot_general | solution.py:102
  217.5 15.3 %convolution_bitcast_fusion = f32[16,2,64,2048]{3,2,0,1:T(8,128)} fusion(f32[2,16,64,176]{3,2,1,0:T(8,128)} %fusion.2, bf16[16,2,64,2048]{3,2,1,0:T(8,128)(2,1)} %all-to-all-done.1, bf16[2,176,2048]{2,1,0:T(8,128)(2,1)} %param.23, bf16[2,2048,176]{1,2,0:T(8,128)(2,1)} %param.22), kind=kOutput, calls=%fused_computation.9 | convolution fusion | flops 2954952704 | bytes 29491200 | tf_op jit(solution)/shard_map/sexf,efd->sexd/dot_general | solution.py:109
  232.9 0.2 reduce-scatter.5.cloned.1.call-start
  233.1 0.1 broadcast_in_dim.137
  233.2 0.1 broadcast_in_dim.138
  233.2 0.3 copy-done.4
  233.5 0.1 copy.56
  233.6 0.1 reduce.2
  233.8 0.6 gather_fusion.3
  234.4 0.1 convert_reduce_fusion.1
  234.4 0.1 select_reduce_fusion.2
  234.5 0.1 bitcast_select_fusion
  234.6 0.4 fusion.37
  235.0 0.0 all-gather.9.cloned.1.call-done
  235.1 1.7 fusion.20
  236.8 0.0 all-gather.7.cloned.1.call-done
  236.8 3.7 fusion.36
  240.5 8.3 %all-gather.5.cloned.1.call-done = bf16[2048,704]{0,1:T(8,128)(2,1)} async-done(((bf16[128,704]{0,1:T(8,128)(2,1)}), bf16[2048,704]{0,1:T(8,128)(2,1)}) %all-gather.5.cloned.1.call-update) | async-done | bytes 2883600 | tf_op jit(solution)/shard_map/all_gather | solution.py:76
  248.8 3.6 fusion.35
  252.4 48.2 %all-gather.11.cloned.1.call-done = bf16[704,2048]{1,0:T(8,128)(2,1)} async-done(((bf16[704,128]{1,0:T(8,128)(2,1)}), bf16[704,2048]{1,0:T(8,128)(2,1)}) %all-gather.11.cloned.1.call-update) | async-done | bytes 2883600 | tf_op jit(solution)/shard_map/all_gather | solution.py:89
  300.7 4.9 %convolution_multiply_fusion = f32[256,2048]{1,0:T(8,128)} fusion(bf16[704,2048]{1,0:T(8,128)(2,1)} %all-gather.11.cloned.1.call-done, f32[256,704]{0,1:T(8,128)} %fusion.36, bf16[256,256]{0,1:T(8,128)(2,1)S(1)} %fusion.20, bf16[256,704]{1,0:T(8,128)(2,1)S(1)} %bitcast_select_fusion, f32[256]{0:T(256)S(1)} %add_divide_fusion, f32[256,704]{0,1:T(8,128)} %fusion.35), kind=kOutput, calls=%fused_computation.10 | convolution fusion | flops 832438272 | bytes 6915072 | tf_op jit(solution)/shard_map/dot_general | solution.py:87
  305.6 88.8 %reduce-scatter.3.cloned.1.call-done = f32[16,2,64,256]{3,2,0,1:T(8,128)} async-done(((f32[16,2,64,2048]{3,2,0,1:T(8,128)}), f32[16,2,64,256]{3,2,0,1:T(8,128)}) %reduce-scatter.3.cloned.1.call-update) | async-done | bytes 2097168 | tf_op jit(solution)/shard_map/reduce_scatter | solution.py:113
  394.4 3.2 copy.54
  397.6 7.0 %all-to-all-start.2 = ((f32[16,2,64,256]{3,2,1,0:T(8,128)}), f32[16,2,64,256]{3,2,1,0:T(8,128)}, u32[]{:S(2)}, u32[]{:S(2)}) async-start(f32[16,2,64,256]{3,2,1,0:T(8,128)} %copy.54), calls=%async_computation.3 | async-start | bytes 4194304 | tf_op jit(solution)/shard_map/all_to_all | solution.py:116
  404.6 0.1 convert_subtract_fusion
  404.7 0.2 copy.51
  404.9 0.1 copy.55
  405.0 0.1 reshape.175
  405.2 0.4 fusion.34
  405.7 0.1 copy.48
  405.8 27.9 %all-to-all-done.2 = f32[16,2,64,256]{3,2,1,0:T(8,128)} async-done(((f32[16,2,64,256]{3,2,1,0:T(8,128)}), f32[16,2,64,256]{3,2,1,0:T(8,128)}, u32[]{:S(2)}, u32[]{:S(2)}) %all-to-all-start.2) | async-done | bytes 2097184 | tf_op jit(solution)/shard_map/all_to_all | solution.py:116
  433.7 5.1 %gather_fusion.1 = f32[1024,256]{1,0:T(8,128)S(1)} fusion(f32[2048,256]{1,0:T(8,128)} %bitcast.15, s32[1024]{0:T(1024)S(1)} %broadcast_clamp_fusion.1), kind=kCustom, calls=%fused_computation.1 | custom fusion | bytes 2101248 | tf_op jit(solution)/shard_map/jit(_take)/gather | solution.py:118
  438.7 1.3 reshape.174
  440.0 2.5 multiply_reduce_fusion
  442.6 0.0 reduce-scatter.5.cloned.1.call-done
  442.6 1.7 add.77
  (34 shorter events, 0.4 us)
Async XLA Ops:
  6.5 227.2 %copy-start = (bf16[64,16,704]{2,1,0:T(8,128)(2,1)S(1)}, bf16[64,16,704]{2,1,0:T(8,128)(2,1)}, u32[]{:S(2)}) copy-start(bf16[64,16,704]{2,1,0:T(8,128)(2,1)} %param.25) | copy-start | bytes 4325380
  6.5 228.5 %all-gather.9.cloned.1.call-start = ((), (), s32[]{:S(2)}) async-start(), calls=%async_computation.8 | async-start | bytes 1179648 | tf_op jit(solution)/shard_map/all_gather | solution.py:61
  8.0 11.3 %copy-start.3 = (s32[256,4]{0,1:T(4,128)S(1)}, s32[256,4]{0,1:T(4,128)}, u32[]{:S(2)}) copy-start(s32[256,4]{0,1:T(4,128)} %param.26) | copy-start | bytes 12292
  10.4 226.4 %all-gather.7.cloned.1.call-start = ((), (), s32[]{:S(2)}) async-start(), calls=%async_computation.7 | async-start | bytes 3063808 | tf_op jit(solution)/shard_map/all_gather | solution.py:81
  13.1 24.3 %all-to-all-start = ((bf16[8,256,256]{2,1,0:T(8,128)(2,1)}), bf16[8,256,256]{2,1,0:T(8,128)(2,1)S(1)}, u32[]{:S(2)}, u32[]{:S(2)}) async-start(bf16[8,256,256]{2,1,0:T(8,128)(2,1)} %stack.2), calls=%async_computation | async-start | bytes 2097152 | tf_op jit(solution)/shard_map/all_to_all | solution.py:27
  18.5 230.3 %all-gather.5.cloned.1.call-start = ((), (), s32[]{:S(2)}) async-start(), calls=%async_computation.6 | async-start | bytes 3063808 | tf_op jit(solution)/shard_map/all_gather | solution.py:76
  37.3 1.0 copy-start.1
  58.2 151.9 %all-to-all-start.1 = ((bf16[16,2,64,2048]{3,2,1,0:T(8,128)(2,1)}), bf16[16,2,64,2048]{3,2,1,0:T(8,128)(2,1)}, u32[]{:S(2)}, u32[]{:S(2)}) async-start(bf16[16,2,64,2048]{3,2,1,0:T(8,128)(2,1)} %select_select_fusion), calls=%async_computation.1 | async-start | bytes 16777216 | tf_op jit(solution)/shard_map/all_to_all | solution.py:101
  65.3 235.4 %all-gather.11.cloned.1.call-start = ((), (), s32[]{:S(2)}) async-start(), calls=%async_computation.9 | async-start | bytes 3063808 | tf_op jit(solution)/shard_map/all_gather | solution.py:89
  65.8 328.5 %reduce-scatter.3.cloned.1.call-start = ((), (), s32[]{:S(2)}) async-start(), calls=%async_computation.5 | async-start | bytes 18874368 | tf_op jit(solution)/shard_map/reduce_scatter | solution.py:113
  232.8 0.7 copy-start.4
  232.8 0.7 copy-start.5
  232.8 1.6 copy-start.6
  232.9 209.7 %reduce-scatter.5.cloned.1.call-start = ((), (), s32[]{:S(2)}) async-start(), calls=%async_computation.10 | async-start | bytes 2359296 | tf_op jit(solution)/shard_map/reduce_scatter | solution.py:114
  397.5 7.6 %copy-start.2 = (bf16[2048,32]{0,1:T(8,128)(2,1)S(1)}, bf16[2048,32]{0,1:T(8,128)(2,1)}, u32[]{:S(2)}) copy-start(bf16[2048,32]{0,1:T(8,128)(2,1)} %param.16) | copy-start | bytes 393220
  397.6 36.1 %all-to-all-start.2 = ((f32[16,2,64,256]{3,2,1,0:T(8,128)}), f32[16,2,64,256]{3,2,1,0:T(8,128)}, u32[]{:S(2)}, u32[]{:S(2)}) async-start(f32[16,2,64,256]{3,2,1,0:T(8,128)} %copy.54), calls=%async_computation.3 | async-start | bytes 4194304 | tf_op jit(solution)/shard_map/all_to_all | solution.py:116
Sparse Core Ops, SparseCore 0:
  10.5 29.7 all-gather.8
  42.4 128.9 all-gather.6
  173.6 75.2 all-gather.4
  250.8 49.8 all-gather.10
  303.0 91.3 reduce-scatter.2
  396.6 34.4 reduce-scatter.4
